TPU v7x, 256 devices: a whole 4x4x8 slice. The times are simulated.
256 devices in a mesh: dp: 32 (over x, y, core), head: 8 (over z).
Axes of the slice: x: 4, y: 4, z: 8, core: 2. Of those that a mesh axis runs over, the one named last changes fastest.
Arguments:
- hidden: bfloat16 [16384, 2048], P('dp'), may hold values from -9 to 9
- parents: int32 [256, 64], P('dp'), may hold values from -1 to 62, as said below
- owner_slot: int32 [256], replicated, may hold values from 0 to 255, as said below
- slot_lengths: int32 [256], P('dp'), may hold values from 65 to 496, as said below
- accepted_path: int32 [256, 16], P('dp'), may hold values from 0 to 63, as said below
- accepted_count: int32 [256], P('dp'), may hold values from 1 to 16, as said below
- cache_keys: bfloat16 [256, 512, 2048], P('dp', None, 'head'), may hold values from -82 to 82
- cache_values: bfloat16 [256, 512, 2048], P('dp', None, 'head'), may hold values from -5 to 5
- w_query: bfloat16 [2048, 2048], P(None, 'head'), may hold values from -0.125 to 0.125
- b_query: float32 [2048], P('head'), may hold values from -3 to 3
- w_key: bfloat16 [2048, 2048], P(None, 'head'), may hold values from -0.25 to 0.25
- w_value: bfloat16 [2048, 2048], P(None, 'head'), may hold values from -0.125 to 0.125
- b_value: float32 [2048], P('head'), may hold values from -3 to 3
- w_out: bfloat16 [2048, 2048], P('head'), may hold values from -0.5 to 0.5
- b_out: float32 [2048], replicated, may hold values from -3 to 3
- first_gain: float32 [2048], replicated, may hold values from 0.48 to 2.25
- first_shift: float32 [2048], replicated, may hold values from -2 to 2
- w_up: bfloat16 [2048, 4096], P(None, 'head'), may hold values from -0.125 to 0.125
- b_up: float32 [4096], P('head'), may hold values from -3 to 3
- w_down: bfloat16 [4096, 2048], P('head'), may hold values from -0.09375 to 0.09375
- b_down: float32 [2048], replicated, may hold values from -3 to 3
- second_gain: float32 [2048], replicated, may hold values from 0.5 to 1.5
- second_shift: float32 [2048], replicated, may hold values from -2 to 2
Outputs:
- layer_out: bfloat16 [16384, 2048], P('dp', 'head')
- new_keys: bfloat16 [256, 16, 2048], P('dp', None, 'head')
- new_values: bfloat16 [256, 16, 2048], P('dp', None, 'head')
Inputs may be any that keep to these rules, and one draw needn't show every extreme that they name: owner_slot is a permutation of the 256 slots; slot s lies on dp index s // 8. Of the 8 requests of one dp index, at most 2 have their slots on one dp index, and on every dp index some 2 do. `slot_lengths`: some slot is filled to exactly 496 positions. parents[r, 0] = -1 and 0 <= parents[r, i] < i for i >= 1. For k < accepted_count[r], accepted_path[r, k] is the node at depth k on the way from the root to some node of request r's tree (so entry 0 is node 0); later entries are arbitrary node indices. `accepted_count`: some request has the full 16 entries.
All inputs are finite; a program needn't handle non-finite values.
Results may differ from a plain program's by a relative error of at most 0.018.
Values may be sent and summed in bfloat16 or wider, within the bound.
No kernel may reach another device: no remote copies, remote signals or barrier semaphores. Data moves between devices by JAX's collectives and lax.ppermute only.
A program may use at most 64 MiB of HBM per device.

v0:
```python
import math
import jax
import jax.numpy as jnp
from jax import lax
from jax.sharding import PartitionSpec as P

HD = 128
PEER_MOST = 2
EPSILON = 1e-05


def ancestry(parent_row, draft):
    nodes = jnp.arange(draft, dtype=jnp.int32)
    reach = (parent_row[:, None] == nodes[None, :]).astype(jnp.float32) + jnp.eye(
        draft, dtype=jnp.float32
    )
    for turn in range(max(1, draft.bit_length())):
        reach = jnp.minimum(jnp.dot(reach, reach, precision=lax.Precision.HIGHEST), 1.0)
    return reach > 0.5


def normalize(mixed, gain, shift):
    center = jnp.mean(mixed, axis=-1, keepdims=True)
    square = jnp.mean(mixed * mixed, axis=-1, keepdims=True)
    return (mixed - center) * lax.rsqrt(square - center * center + EPSILON) * gain + shift


def normalize_shared(mixed, sums, gain, shift, model_width):
    center = (sums[0] / model_width)[:, None]
    square = (sums[1] / model_width)[:, None]
    return (mixed - center) * lax.rsqrt(square - center * center + EPSILON) * gain + shift


def split_three(values):
    high = values.astype(jnp.bfloat16)
    rest = values - high.astype(jnp.float32)
    middle = rest.astype(jnp.bfloat16)
    low = (rest - middle.astype(jnp.float32)).astype(jnp.bfloat16)
    return jnp.stack([high, middle, low], axis=1)


def join_three(pieces):
    wide = pieces.astype(jnp.float32)
    return wide[:, 0] + (wide[:, 1] + wide[:, 2])


def local(
    hidden,
    parents,
    owner_slot,
    slot_lengths,
    accepted_path,
    accepted_count,
    cache_keys,
    cache_values,
    w_query,
    b_query,
    w_key,
    w_value,
    b_value,
    w_out,
    b_out,
    first_gain,
    first_shift,
    w_up,
    b_up,
    w_down,
    b_down,
    second_gain,
    second_shift,
):
    requests = parents.shape[0]
    draft = parents.shape[1]
    tokens = hidden.shape[0]
    model_width = hidden.shape[1]
    width = w_query.shape[1]
    local_heads = width // HD
    capacity = cache_keys.shape[1]
    block = min(capacity, 256)
    shards = lax.axis_size("dp")
    myself = lax.axis_index("dp")
    scale = 1.0 / math.sqrt(HD)
    queries = (jnp.dot(hidden, w_query, preferred_element_type=jnp.float32) + b_query).astype(
        jnp.bfloat16
    )
    key_rows = jnp.dot(hidden, w_key, preferred_element_type=jnp.float32).astype(jnp.bfloat16)
    value_rows = (jnp.dot(hidden, w_value, preferred_element_type=jnp.float32) + b_value).astype(
        jnp.bfloat16
    )
    local_ids = jnp.arange(requests, dtype=jnp.int32)
    levels = jnp.arange(accepted_path.shape[1], dtype=jnp.int32)
    chosen = local_ids[:, None] * draft + accepted_path
    usable = (levels[None, :] < accepted_count[:, None])[..., None]
    kept_keys = jnp.where(usable, key_rows[chosen], jnp.zeros((), jnp.bfloat16))
    kept_values = jnp.where(usable, value_rows[chosen], jnp.zeros((), jnp.bfloat16))
    tree_queries = queries.reshape(requests, draft, local_heads, HD)
    tree_keys = key_rows.reshape(requests, draft, local_heads, HD)
    tree_values = value_rows.reshape(requests, draft, local_heads, HD)
    lineage = jax.vmap(lambda parent_row: ancestry(parent_row, draft))(parents)
    tree_scores = (
        jnp.einsum("rqhd,rkhd->rhqk", tree_queries, tree_keys, preferred_element_type=jnp.float32)
        * scale
    )
    tree_scores = jnp.where(lineage[:, None], tree_scores, -jnp.inf)
    tree_top = jnp.max(tree_scores, axis=3, keepdims=True)
    tree_exp = jnp.exp(tree_scores - tree_top)
    tree_total = jnp.sum(tree_exp, axis=3, keepdims=True)
    tree_probs = tree_exp.astype(jnp.bfloat16)
    tree_part = jnp.einsum(
        "rhqk,rkhd->rqhd", tree_probs, tree_values, preferred_element_type=jnp.float32
    ) / jnp.transpose(tree_total, (0, 2, 1, 3))
    tree_lse = jnp.transpose((tree_top + jnp.log(tree_total))[..., 0], (0, 2, 1))[..., None]
    my_owner = lax.dynamic_slice_in_dim(owner_slot, myself * requests, requests)
    target = my_owner // requests
    earlier = local_ids[None, :] < local_ids[:, None]
    same_target = target[None, :] == target[:, None]
    rank = jnp.sum((earlier & same_target).astype(jnp.int32), axis=1)
    my_slots = myself * requests + local_ids
    every_id = jnp.arange(owner_slot.shape[0], dtype=jnp.int32)
    source_request = jnp.sum(
        jnp.where(owner_slot[None, :] == my_slots[:, None], every_id[None, :], 0), axis=1
    )
    source = source_request // requests
    source_local = source_request % requests
    source_targets = owner_slot.reshape(shards, requests)[source] // requests
    source_rank = jnp.sum(
        ((local_ids[None, :] < source_local[:, None]) & (source_targets == myself)).astype(
            jnp.int32
        ),
        axis=1,
    )
    shaped_queries = queries.reshape(requests, draft, width)
    slots_total = shards * PEER_MOST
    send_index = target * PEER_MOST + rank
    receive_index = source * PEER_MOST + source_rank
    slot_ids = jnp.arange(slots_total, dtype=jnp.int32)

    def spread(values, index):
        placing = (index[None, :] == slot_ids[:, None]).astype(values.dtype)
        flat = values.reshape(values.shape[0], -1)
        placed = jnp.dot(placing, flat, preferred_element_type=jnp.float32).astype(values.dtype)
        return placed.reshape((slots_total,) + values.shape[1:])

    arrived = lax.all_to_all(
        spread(shaped_queries, send_index), "dp", split_axis=0, concat_axis=0, tiled=True
    )
    kept = lax.all_to_all(
        spread(jnp.concatenate([kept_keys, kept_values], axis=1), send_index),
        "dp",
        split_axis=0,
        concat_axis=0,
        tiled=True,
    )[receive_index]
    owned_queries = arrived[receive_index].reshape(requests, draft, local_heads, HD)
    new_keys = kept[:, : kept_keys.shape[1]]
    new_values = kept[:, kept_keys.shape[1] :]
    slot_keys = cache_keys.reshape(requests, capacity, local_heads, HD)
    slot_values = cache_values.reshape(requests, capacity, local_heads, HD)
    scores = (
        jnp.einsum("sqhd,skhd->shqk", owned_queries, slot_keys, preferred_element_type=jnp.float32)
        * scale
    )
    living = jnp.arange(capacity, dtype=jnp.int32)[None, :] < slot_lengths[:, None]
    scores = jnp.where(living[:, None, None, :], scores, -jnp.inf)
    cache_top = jnp.max(scores, axis=3, keepdims=True)
    cache_exp = jnp.exp(scores - cache_top)
    cache_total = jnp.sum(cache_exp, axis=3, keepdims=True)
    cache_probs = cache_exp.astype(jnp.bfloat16)
    gathered = jnp.einsum(
        "shqk,skhd->sqhd", cache_probs, slot_values, preferred_element_type=jnp.float32
    )
    owned_part = (
        (gathered / jnp.transpose(cache_total, (0, 2, 1, 3)))
        .astype(jnp.bfloat16)
        .reshape(requests, draft, width)
    )
    owned_lse = (cache_top + jnp.log(cache_total))[..., 0]
    lse_flat = split_three(owned_lse).reshape(requests, -1)
    lse_rows = -(-lse_flat.shape[1] // width)
    lse_flat = jnp.pad(lse_flat, ((0, 0), (0, lse_rows * width - lse_flat.shape[1])))
    back = jnp.concatenate(
        [
            spread(owned_part, receive_index),
            spread(lse_flat, receive_index).reshape(slots_total, lse_rows, width),
        ],
        axis=1,
    )
    returned = lax.all_to_all(back, "dp", split_axis=0, concat_axis=0, tiled=True)[send_index]
    cache_part = returned[:, :draft]
    lse_back = returned[:, draft:].reshape(requests, -1)[:, : 3 * local_heads * draft]
    cache_lse = join_three(lse_back.reshape(requests, 3, local_heads, draft))
    cache_weight = jnp.transpose(cache_lse, (0, 2, 1))[..., None]
    larger = jnp.maximum(cache_weight, tree_lse)
    cache_share = jnp.exp(cache_weight - larger)
    tree_share = jnp.exp(tree_lse - larger)
    blended = (
        cache_share * cache_part.astype(jnp.float32).reshape(requests, draft, local_heads, HD)
        + tree_share * tree_part
    ) / (cache_share + tree_share)
    attended = blended.astype(jnp.bfloat16).reshape(tokens, width)
    attention_term = jnp.dot(attended, w_out, preferred_element_type=jnp.float32)
    feature = model_width // lax.axis_size("head")
    offset = lax.axis_index("head") * feature

    def columns(values):
        return lax.dynamic_slice_in_dim(values, offset, feature, values.ndim - 1)

    attention_sum = lax.psum(attention_term.astype(jnp.bfloat16), "head").astype(jnp.float32)
    first_normed = normalize(
        attention_sum + b_out + hidden.astype(jnp.float32), first_gain, first_shift
    ).astype(jnp.bfloat16)
    inner = jax.nn.gelu(
        jnp.dot(first_normed, w_up, preferred_element_type=jnp.float32) + b_up, approximate=True
    ).astype(jnp.bfloat16)
    down_share = lax.psum_scatter(
        jnp.dot(inner, w_down, preferred_element_type=jnp.float32).astype(jnp.bfloat16),
        "head",
        scatter_dimension=1,
        tiled=True,
    ).astype(jnp.float32)
    second_mixed = down_share + columns(b_down) + columns(first_normed).astype(jnp.float32)
    heads_along = lax.axis_size("head")
    own_sums = jnp.stack(
        [jnp.sum(second_mixed, axis=1), jnp.sum(second_mixed * second_mixed, axis=1)]
    )
    second_sums = jnp.sum(
        lax.all_to_all(
            jnp.broadcast_to(own_sums[None], (heads_along,) + own_sums.shape),
            "head",
            0,
            0,
            tiled=False,
        ),
        axis=0,
    )
    layer_out = normalize_shared(
        second_mixed, second_sums, columns(second_gain), columns(second_shift), model_width
    ).astype(jnp.bfloat16)
    return (layer_out, new_keys, new_values)


def solution(mesh):
    placed = (
        P("dp", None),
        P("dp", None),
        P(),
        P("dp"),
        P("dp", None),
        P("dp"),
        P("dp", None, "head"),
        P("dp", None, "head"),
        P(None, "head"),
        P("head"),
        P(None, "head"),
        P(None, "head"),
        P("head"),
        P("head", None),
        P(),
        P(),
        P(),
        P(None, "head"),
        P("head"),
        P("head", None),
        P(),
        P(),
        P(),
    )
    return jax.shard_map(
        local,
        mesh=mesh,
        in_specs=placed,
        out_specs=(P("dp", "head"), P("dp", None, "head"), P("dp", None, "head")),
        check_vma=False,
    )
```

profile of v0, /device:TPU:2, one launch (start us, length us, event | category | flops | bytes accessed | tf_op | source)
XLA Modules:
  0.0 265.0 jit_solution(14753216439915072856)
XLA Ops:
  7.2 0.9 and_select_fusion
  8.1 0.2 convert_reduce_fusion
  8.3 0.8 compare_select_fusion.1
  9.0 2.6 fusion.24
  11.8 0.7 convolution_convert_fusion.1
  12.5 1.8 copy.75
  14.3 7.8 %all-to-all-start = ((bf16[64,64,256]{2,1,0:T(8,128)(2,1)}), bf16[64,64,256]{2,1,0:T(8,128)(2,1)}, u32[]{:S(2)}, u32[]{:S(2)}) async-start(bf16[64,64,256]{2,1,0:T(8,128)(2,1)} %bitcast.164), calls=%async_computation | async-start | bytes 4194304 | tf_op jit(solution)/shard_map/all_to_all | solution.py:144
  22.2 0.2 select_reduce_fusion
  22.5 0.6 gather_fusion
  23.0 0.2 convert_reduce_fusion.1
  23.4 0.5 convolution_minimum_fusion.6
  23.9 2.6 convolution_convert_fusion.5
  26.5 21.7 %all-to-all-done = bf16[64,64,256]{2,1,0:T(8,128)(2,1)} async-done(((bf16[64,64,256]{2,1,0:T(8,128)(2,1)}), bf16[64,64,256]{2,1,0:T(8,128)(2,1)}, u32[]{:S(2)}, u32[]{:S(2)}) %all-to-all-start) | async-done | bytes 2097184 | tf_op jit(solution)/shard_map/all_to_all | solution.py:144
  48.1 2.2 gather_fusion.1
  50.3 2.5 fusion.7
  52.8 0.7 fusion.8
  53.6 0.9 copy-done.11
  54.4 0.9 fusion.21
  55.3 0.3 copy.58
  55.6 0.2 reshape_reshape.7
  55.8 0.7 convolution_convert_fusion
  56.5 1.9 copy.76
  58.4 0.1 convolution_convert_fusion.6
  58.6 3.2 %pad_maximum_fusion = bf16[64,66,256]{2,1,0:T(8,128)(2,1)} fusion(bf16[64,2,256]{2,1,0:T(2,128)(2,1)S(1)} %reshape.370, bf16[64,64,256]{2,1,0:T(8,128)(2,1)} %bitcast.165), kind=kLoop, calls=%fused_computation.15 | loop fusion | flops 4325376 | bytes 4325376 | tf_op jit(solution)/shard_map/concatenate | solution.py:181
  61.8 7.6 %all-to-all-start.1 = ((bf16[64,66,256]{2,1,0:T(8,128)(2,1)}), bf16[64,66,256]{2,1,0:T(8,128)(2,1)}, u32[]{:S(2)}, u32[]{:S(2)}) async-start(bf16[64,66,256]{2,1,0:T(8,128)(2,1)} %pad_maximum_fusion), calls=%async_computation.1 | async-start | bytes 4718592 | tf_op jit(solution)/shard_map/all_to_all | solution.py:188
  69.5 0.2 all-reduce.3.cloned.1.call-start
  69.7 0.4 convolution_minimum_fusion.5
  70.2 0.8 reshape.373
  70.9 0.4 convolution_minimum_fusion.4
  71.3 0.4 convolution_minimum_fusion.3
  71.7 0.4 convolution_minimum_fusion.2
  72.1 0.4 convolution_minimum_fusion.1
  72.5 0.4 fusion.27
  72.9 0.2 copy.59
  73.1 2.6 fusion.25
  75.7 0.8 reshape.376
  76.5 1.2 fusion.91
  77.8 20.6 %all-to-all-done.1 = bf16[64,66,256]{2,1,0:T(8,128)(2,1)} async-done(((bf16[64,66,256]{2,1,0:T(8,128)(2,1)}), bf16[64,66,256]{2,1,0:T(8,128)(2,1)}, u32[]{:S(2)}, u32[]{:S(2)}) %all-to-all-start.1) | async-done | bytes 2162720 | tf_op jit(solution)/shard_map/all_to_all | solution.py:188
  98.4 2.2 gather_fusion.2
  100.8 1.8 fusion.26
  102.6 0.3 copy.65
  102.9 2.0 convolution_convert_fusion.3
  105.0 83.3 %all-reduce.3.cloned.1.call-done = bf16[512,2048]{1,0:T(8,128)(2,1)} async-done(((bf16[512,2048]{1,0:T(8,128)(2,1)}), bf16[512,2048]{1,0:T(8,128)(2,1)}) %all-reduce.3.cloned.1.call-update) | async-done | bytes 2097168 | tf_op jit(solution)/shard_map/psum | solution.py:208
  188.3 3.5 %fusion = (f32[512]{0:T(512)S(1)}, f32[512]{0:T(512)S(1)}) fusion(bf16[512,2048]{1,0:T(8,128)(2,1)} %param.23, bf16[512,2048]{1,0:T(8,128)(2,1)} %all-reduce.3.cloned.1.call-done, f32[2048]{0:T(1024)S(1)} %copy-done.4), kind=kLoop, calls=%fused_computation.12 | loop fusion | flops 7339008 | bytes 4206592 | tf_op jit(solution)/shard_map/reduce_sum | solution.py:23
  191.8 2.6 add_convert_fusion
  194.5 6.1 %convolution_convert_fusion.4 = bf16[512,2048]{1,0:T(8,128)(2,1)} fusion(bf16[512,2048]{1,0:T(8,128)(2,1)S(1)} %copy-done, bf16[512,2048]{1,0:T(8,128)(2,1)} %add_convert_fusion, bf16[2048,512]{1,0:T(8,128)(2,1)} %param.40, f32[512]{0:T(512)S(1)} %copy-done.12), kind=kOutput, calls=%fused_computation.14 | convolution fusion | flops 2151153664 | bytes 8390656 | tf_op jit(solution)/shard_map/dot_general | solution.py:216
  200.6 0.6 copy-done.9
  201.4 0.8 gather_fusion.3
  202.2 0.8 gather_fusion.4
  203.4 0.4 convolution_convert_fusion.2
  203.8 1.2 copy.80
  205.0 7.4 %all-to-all-start.3 = ((bf16[64,32,256]{2,1,0:T(8,128)(2,1)}), bf16[64,32,256]{2,1,0:T(8,128)(2,1)S(1)}, u32[]{:S(2)}, u32[]{:S(2)}) async-start(bf16[64,32,256]{2,1,0:T(8,128)(2,1)} %bitcast.47), calls=%async_computation.4 | async-start | bytes 2097152 | tf_op jit(solution)/shard_map/all_to_all | solution.py:147
  212.5 0.8 dynamic_slice.16
  213.2 0.8 dynamic_slice.18
  214.0 0.8 dynamic_slice.19
  214.7 12.1 %all-to-all-done.3 = bf16[64,32,256]{2,1,0:T(8,128)(2,1)S(1)} async-done(((bf16[64,32,256]{2,1,0:T(8,128)(2,1)}), bf16[64,32,256]{2,1,0:T(8,128)(2,1)S(1)}, u32[]{:S(2)}, u32[]{:S(2)}) %all-to-all-start.3) | async-done | bytes 1048608 | tf_op jit(solution)/shard_map/all_to_all | solution.py:147
  226.9 0.6 gather_fusion.5
  227.5 14.1 %reduce-scatter.2.cloned.1.call-done = bf16[512,256]{1,0:T(8,128)(2,1)} async-done(((bf16[512,2048]{1,0:T(8,128)(2,1)}), bf16[512,256]{1,0:T(8,128)(2,1)}) %reduce-scatter.2.cloned.1.call-update) | async-done | bytes 262160 | tf_op jit(solution)/shard_map/reduce_scatter | solution.py:215
  241.6 1.3 fusion.48
  242.9 0.6 broadcast_in_dim.71
  243.5 4.7 %all-to-all-start.2 = ((f32[8,2,512]{2,1,0:T(2,128)}), f32[8,2,512]{2,1,0:T(2,128)S(1)}, u32[]{:S(2)}, u32[]{:S(2)}) async-start(f32[8,2,512]{2,1,0:T(2,128)} %broadcast_in_dim.71), calls=%async_computation.3 | async-start | bytes 65536 | tf_op jit(solution)/shard_map/all_to_all | solution.py:227
  248.2 0.7 fusion.90
  248.8 7.4 %all-to-all-done.2 = f32[8,2,512]{2,1,0:T(2,128)S(1)} async-done(((f32[8,2,512]{2,1,0:T(2,128)}), f32[8,2,512]{2,1,0:T(2,128)S(1)}, u32[]{:S(2)}, u32[]{:S(2)}) %all-to-all-start.2) | async-done | bytes 32800 | tf_op jit(solution)/shard_map/all_to_all | solution.py:227
  256.3 1.9 add_convert_fusion.1
  (68 shorter events, 1.5 us)
Async XLA Ops:
  7.2 187.3 %copy-start = (bf16[512,2048]{1,0:T(8,128)(2,1)S(1)}, bf16[512,2048]{1,0:T(8,128)(2,1)}, u32[]{:S(2)}) copy-start(bf16[512,2048]{1,0:T(8,128)(2,1)} %param.42) | copy-start | bytes 6291460
  14.3 7.8 %copy-start.7 = (s32[256]{0:T(256)S(1)}, s32[256]{0:T(256)}, u32[]{:S(2)}) copy-start(s32[256]{0:T(256)} %param.25) | copy-start | bytes 3076
  14.3 9.0 %copy-start.10 = (s32[8]{0:T(128)S(1)}, s32[8]{0:T(128)}, u32[]{:S(2)}) copy-start(s32[8]{0:T(128)} %param.26) | copy-start | bytes 100
  14.3 9.0 %copy-start.8 = (s32[8,64]{1,0:T(8,128)S(1)}, s32[8,64]{1,0:T(8,128)}, u32[]{:S(2)}) copy-start(s32[8,64]{1,0:T(8,128)} %param.24) | copy-start | bytes 6148
  14.3 33.8 %all-to-all-start = ((bf16[64,64,256]{2,1,0:T(8,128)(2,1)}), bf16[64,64,256]{2,1,0:T(8,128)(2,1)}, u32[]{:S(2)}, u32[]{:S(2)}) async-start(bf16[64,64,256]{2,1,0:T(8,128)(2,1)} %bitcast.164), calls=%async_computation | async-start | bytes 4194304 | tf_op jit(solution)/shard_map/all_to_all | solution.py:144
  52.8 1.6 copy-start.11
  61.8 36.6 %all-to-all-start.1 = ((bf16[64,66,256]{2,1,0:T(8,128)(2,1)}), bf16[64,66,256]{2,1,0:T(8,128)(2,1)}, u32[]{:S(2)}, u32[]{:S(2)}) async-start(bf16[64,66,256]{2,1,0:T(8,128)(2,1)} %pad_maximum_fusion), calls=%async_computation.1 | async-start | bytes 4718592 | tf_op jit(solution)/shard_map/all_to_all | solution.py:188
  69.5 118.8 %all-reduce.3.cloned.1.call-start = ((), (), s32[]{:S(2)}) async-start(), calls=%async_computation.5 | async-start | bytes 4194304 | tf_op jit(solution)/shard_map/psum | solution.py:208
  70.2 2.9 %copy-start.13 = (f32[256]{0:T(256)S(1)}, f32[256]{0:T(256)}, u32[]{:S(2)}) copy-start(f32[256]{0:T(256)} %param.35) | copy-start | bytes 3076
  100.8 2.1 copy-start.3
  102.9 85.4 %copy-start.4 = (f32[2048]{0:T(1024)S(1)}, f32[2048]{0:T(1024)}, u32[]{:S(2)}) copy-start(f32[2048]{0:T(1024)} %param.37) | copy-start | bytes 24580
  104.9 86.9 %copy-start.5 = (f32[2048]{0:T(1024)S(1)}, f32[2048]{0:T(1024)}, u32[]{:S(2)}) copy-start(f32[2048]{0:T(1024)} %param.39) | copy-start | bytes 24580
  105.0 86.8 %copy-start.6 = (f32[2048]{0:T(1024)S(1)}, f32[2048]{0:T(1024)}, u32[]{:S(2)}) copy-start(f32[2048]{0:T(1024)} %param.38) | copy-start | bytes 24580
  105.0 136.6 %reduce-scatter.2.cloned.1.call-start = ((), (), s32[]{:S(2)}) async-start(), calls=%async_computation.6 | async-start | bytes 2359296 | tf_op jit(solution)/shard_map/reduce_scatter | solution.py:215
  188.3 3.5 %copy-start.1 = (bf16[512,2048]{1,0:T(8,128)(2,1)S(1)}, bf16[512,2048]{1,0:T(8,128)(2,1)}, u32[]{:S(2)}) copy-start(bf16[512,2048]{1,0:T(8,128)(2,1)} %param.23) | copy-start | bytes 6291460
  188.3 3.5 %copy-start.2 = (bf16[512,2048]{1,0:T(8,128)(2,1)S(1)}, bf16[512,2048]{1,0:T(8,128)(2,1)}, u32[]{:S(2)}) copy-start(bf16[512,2048]{1,0:T(8,128)(2,1)} %all-reduce.3.cloned.1.call-done) | copy-start | bytes 6291460
  191.8 2.6 copy-start.12
  200.5 0.7 copy-start.9
  200.5 2.6 copy-start.14
  205.0 21.9 %all-to-all-start.3 = ((bf16[64,32,256]{2,1,0:T(8,128)(2,1)}), bf16[64,32,256]{2,1,0:T(8,128)(2,1)S(1)}, u32[]{:S(2)}, u32[]{:S(2)}) async-start(bf16[64,32,256]{2,1,0:T(8,128)(2,1)} %bitcast.47), calls=%async_computation.4 | async-start | bytes 2097152 | tf_op jit(solution)/shard_map/all_to_all | solution.py:147
  243.5 12.7 %all-to-all-start.2 = ((f32[8,2,512]{2,1,0:T(2,128)}), f32[8,2,512]{2,1,0:T(2,128)S(1)}, u32[]{:S(2)}, u32[]{:S(2)}) async-start(f32[8,2,512]{2,1,0:T(2,128)} %broadcast_in_dim.71), calls=%async_computation.3 | async-start | bytes 65536 | tf_op jit(solution)/shard_map/all_to_all | solution.py:227
Sparse Core Ops, SparseCore 0:
  105.1 83.2 all-reduce.2
  200.7 40.8 reduce-scatter.1
where the time goes:
time: 266 us; the launch traced here: 265 us
  waiting for transfers between devices  159 us (60%)
  starting transfers between devices  27.8 us (10%)
  matrix products  27 us (10%)
  local copies, waits for them, and re-layouts  20.3 us (8%)
  other arithmetic  16.1 us (6%)
  between operations  14.6 us (5%)
    psum x1, waiting for transfers between devices, local(): lax.psum(attention_term.astype(jnp.bfloat16), 'head').astype(jnp.float32)  83.3 us
    all_to_all x1, waiting for transfers between devices, local(): lax.all_to_all(spread(shaped_queries, send_index), 'dp', split_axis=0, co...  21.7 us
    all_to_all x1, waiting for transfers between devices, local(): lax.all_to_all(back, 'dp', split_axis=0, concat_axis=0, tiled=True)  20.6 us
    reduce_scatter x1, waiting for transfers between devices, local(): lax.psum_scatter(jnp.dot(inner, w_down, preferred_element_type=jnp.float3...  14.1 us
    all_to_all x1, waiting for transfers between devices, local(): lax.all_to_all(spread(jnp.concatenate([kept_keys, kept_values], axis=1),...  12.1 us
    all_to_all x1, starting transfers between devices, local(): lax.all_to_all(spread(shaped_queries, send_index), 'dp', split_axis=0, co...  7.81 us
    all_to_all x1, starting transfers between devices, local(): lax.all_to_all(back, 'dp', split_axis=0, concat_axis=0, tiled=True)  7.64 us
    all_to_all x1, starting transfers between devices, local(): lax.all_to_all(spread(jnp.concatenate([kept_keys, kept_values], axis=1),...  7.42 us
  transfers between devices with their start and end apart: 6, of which 6 were waited for; matrix products, arithmetic and copies ran while one was open for 7% of the time, Pallas kernels for 0%

commit v1 on v0

--- a/solution.py
+++ b/solution.py
@@ -205,7 +205,9 @@
     def columns(values):
         return lax.dynamic_slice_in_dim(values, offset, feature, values.ndim - 1)
 
-    attention_sum = lax.psum(attention_term.astype(jnp.bfloat16), "head").astype(jnp.float32)
+    attention_sum = jnp.sum(
+        lax.all_gather(attention_term.astype(jnp.bfloat16), "head"), axis=0
+    ).astype(jnp.float32)
     first_normed = normalize(
         attention_sum + b_out + hidden.astype(jnp.float32), first_gain, first_shift
     ).astype(jnp.bfloat16)

time: 266 us -> 365 us (1.37)
  waiting for transfers between devices: 159 us -> 250 us
  other arithmetic: 16.1 us -> 25.3 us
    all_gather x0 -> x1, waiting for transfers between devices: none -> 174 us  [local(): lax.all_gather(attention_term.astype(jnp.bfloat16), 'head')]
    psum x1 -> x0, waiting for transfers between devices: 83.3 us -> none  [local(): lax.psum(attention_term.astype(jnp.bfloat16), 'head').astype(jnp.float32)]
    reduce_sum x0 -> x1, other arithmetic: none -> 10.8 us  [local(): jnp.sum(lax.all_gather(attention_term.astype(jnp.bfloat16), 'head'), axis=0)]
  transfers between devices with their start and end apart: 6 -> 6, of which waited for: 6 -> 6; matrix products, arithmetic and copies ran while one was open for 7% -> 5% of each run, Pallas kernels for 0% -> 0%
where the time goes in v1:
time: 365 us; the launch traced here: 364 us
  waiting for transfers between devices  250 us (68%)
  starting transfers between devices  27.9 us (8%)
  matrix products  27 us (7%)
  other arithmetic  25.3 us (7%)
  local copies, waits for them, and re-layouts  19 us (5%)
  between operations  14.6 us (4%)
    all_gather x1, waiting for transfers between devices, local(): lax.all_gather(attention_term.astype(jnp.bfloat16), 'head')  174 us
    all_to_all x1, waiting for transfers between devices, local(): lax.all_to_all(spread(shaped_queries, send_index), 'dp', split_axis=0, co...  23.9 us
    all_to_all x1, waiting for transfers between devices, local(): lax.all_to_all(back, 'dp', split_axis=0, concat_axis=0, tiled=True)  18.4 us
    reduce_scatter x1, waiting for transfers between devices, local(): lax.psum_scatter(jnp.dot(inner, w_down, preferred_element_type=jnp.float3...  13.9 us
    all_to_all x1, waiting for transfers between devices, local(): lax.all_to_all(spread(jnp.concatenate([kept_keys, kept_values], axis=1),...  12.1 us
    reduce_sum x1, other arithmetic, local(): jnp.sum(lax.all_gather(attention_term.astype(jnp.bfloat16), 'head'), axis=0)  10.8 us
    all_to_all x1, starting transfers between devices, local(): lax.all_to_all(spread(shaped_queries, send_index), 'dp', split_axis=0, co...  7.81 us
    all_to_all x1, starting transfers between devices, local(): lax.all_to_all(back, 'dp', split_axis=0, concat_axis=0, tiled=True)  7.64 us
  transfers between devices with their start and end apart: 6, of which 6 were waited for; matrix products, arithmetic and copies ran while one was open for 5% of the time, Pallas kernels for 0%

profile of v1, /device:TPU:2, one launch (start us, length us, event | category | flops | bytes accessed | tf_op | source)
XLA Modules:
  0.0 363.6 jit_solution(2431267969088998468)
XLA Ops:
  7.2 0.9 and_select_fusion
  8.1 0.2 convert_reduce_fusion
  8.3 0.8 compare_select_fusion.1
  9.0 2.6 fusion.24
  11.8 0.7 convolution_convert_fusion.1
  12.5 1.8 copy.75
  14.3 7.8 %all-to-all-start = ((bf16[64,64,256]{2,1,0:T(8,128)(2,1)}), bf16[64,64,256]{2,1,0:T(8,128)(2,1)}, u32[]{:S(2)}, u32[]{:S(2)}) async-start(bf16[64,64,256]{2,1,0:T(8,128)(2,1)} %bitcast.166), calls=%async_computation | async-start | bytes 4194304 | tf_op jit(solution)/shard_map/all_to_all | solution.py:144
  22.2 0.2 select_reduce_fusion
  22.5 0.6 gather_fusion
  23.0 0.2 convert_reduce_fusion.1
  23.4 0.5 convolution_minimum_fusion.6
  23.9 0.4 convolution_minimum_fusion.5
  24.3 23.9 %all-to-all-done = bf16[64,64,256]{2,1,0:T(8,128)(2,1)} async-done(((bf16[64,64,256]{2,1,0:T(8,128)(2,1)}), bf16[64,64,256]{2,1,0:T(8,128)(2,1)}, u32[]{:S(2)}, u32[]{:S(2)}) %all-to-all-start) | async-done | bytes 2097184 | tf_op jit(solution)/shard_map/all_to_all | solution.py:144
  48.1 2.2 gather_fusion.1
  50.3 2.5 fusion.7
  52.8 0.7 fusion.8
  53.6 0.9 copy-done.11
  54.4 0.9 fusion.21
  55.3 0.3 copy.58
  55.6 0.2 reshape_reshape.7
  56.1 0.7 convolution_convert_fusion
  56.8 0.5 copy.76
  57.3 1.6 pad_maximum_fusion
  58.9 7.6 %all-to-all-start.1 = ((bf16[64,66,256]{2,1,0:T(8,128)(2,1)}), bf16[64,66,256]{2,1,0:T(8,128)(2,1)}, u32[]{:S(2)}, u32[]{:S(2)}) async-start(bf16[64,66,256]{2,1,0:T(8,128)(2,1)} %pad_maximum_fusion), calls=%async_computation.1 | async-start | bytes 4718592 | tf_op jit(solution)/shard_map/all_to_all | solution.py:188
  66.6 0.2 all-gather.3.cloned.1.call-start
  66.8 0.4 convolution_minimum_fusion.4
  67.3 0.4 convolution_minimum_fusion.3
  67.7 0.4 convolution_minimum_fusion.2
  68.0 0.4 convolution_minimum_fusion.1
  68.4 0.4 fusion.27
  69.0 2.6 convolution_convert_fusion.5
  71.6 0.8 reshape.373
  72.4 2.6 fusion.25
  75.0 0.8 reshape.376
  75.7 1.2 fusion.91
  77.1 18.4 %all-to-all-done.1 = bf16[64,66,256]{2,1,0:T(8,128)(2,1)} async-done(((bf16[64,66,256]{2,1,0:T(8,128)(2,1)}), bf16[64,66,256]{2,1,0:T(8,128)(2,1)}, u32[]{:S(2)}, u32[]{:S(2)}) %all-to-all-start.1) | async-done | bytes 2162720 | tf_op jit(solution)/shard_map/all_to_all | solution.py:188
  95.5 2.2 gather_fusion.2
  97.9 1.8 fusion.26
  99.7 0.3 copy.65
  100.0 2.1 convolution_convert_fusion.3
  102.1 0.3 reduce-scatter.2.cloned.1.call-start
  102.4 174.1 %all-gather.3.cloned.1.call-done = bf16[4096,2048]{1,0:T(8,128)(2,1)} async-done(((bf16[512,2048]{1,0:T(8,128)(2,1)}), bf16[4096,2048]{1,0:T(8,128)(2,1)}) %all-gather.3.cloned.1.call-update) | async-done | bytes 16777232 | tf_op jit(solution)/shard_map/all_gather | solution.py:209
  276.4 10.8 %reduce_sum.113 = bf16[512,2048]{1,0:T(8,128)(2,1)} reduce(bf16[8,512,2048]{2,1,0:T(8,128)(2,1)} %bitcast.163, bf16[]{:T(256)} %constant.89.clone.1), dimensions={0}, to_apply=%region_7.8 | reduce | flops 7340032 | bytes 18874370 | tf_op jit(solution)/shard_map/reduce_sum | solution.py:208
  287.2 3.5 fusion
  290.8 2.6 add_convert_fusion
  293.4 6.1 %convolution_convert_fusion.4 = bf16[512,2048]{1,0:T(8,128)(2,1)} fusion(bf16[512,2048]{1,0:T(8,128)(2,1)S(1)} %copy-done, bf16[512,2048]{1,0:T(8,128)(2,1)} %add_convert_fusion, bf16[2048,512]{1,0:T(8,128)(2,1)} %param.40, f32[512]{0:T(512)S(1)} %copy-done.12), kind=kOutput, calls=%fused_computation.14 | convolution fusion | flops 2151153664 | bytes 8390656 | tf_op jit(solution)/shard_map/dot_general | solution.py:218
  299.5 0.6 copy-done.9
  300.3 0.8 gather_fusion.3
  301.2 0.8 gather_fusion.4
  302.3 0.4 convolution_convert_fusion.2
  302.7 1.2 copy.80
  304.0 7.4 %all-to-all-start.3 = ((bf16[64,32,256]{2,1,0:T(8,128)(2,1)}), bf16[64,32,256]{2,1,0:T(8,128)(2,1)S(1)}, u32[]{:S(2)}, u32[]{:S(2)}) async-start(bf16[64,32,256]{2,1,0:T(8,128)(2,1)} %bitcast.48), calls=%async_computation.4 | async-start | bytes 2097152 | tf_op jit(solution)/shard_map/all_to_all | solution.py:147
  311.4 0.8 dynamic_slice.16
  312.1 0.8 dynamic_slice.18
  312.9 0.8 dynamic_slice.19
  313.7 12.1 %all-to-all-done.3 = bf16[64,32,256]{2,1,0:T(8,128)(2,1)S(1)} async-done(((bf16[64,32,256]{2,1,0:T(8,128)(2,1)}), bf16[64,32,256]{2,1,0:T(8,128)(2,1)S(1)}, u32[]{:S(2)}, u32[]{:S(2)}) %all-to-all-start.3) | async-done | bytes 1048608 | tf_op jit(solution)/shard_map/all_to_all | solution.py:147
  325.8 0.6 gather_fusion.5
  326.4 13.9 %reduce-scatter.2.cloned.1.call-done = bf16[512,256]{1,0:T(8,128)(2,1)} async-done(((bf16[512,2048]{1,0:T(8,128)(2,1)}), bf16[512,256]{1,0:T(8,128)(2,1)}) %reduce-scatter.2.cloned.1.call-update) | async-done | bytes 262160 | tf_op jit(solution)/shard_map/reduce_scatter | solution.py:217
  340.3 1.3 fusion.48
  341.5 0.6 broadcast_in_dim.71
  342.2 4.6 %all-to-all-start.2 = ((f32[8,2,512]{2,1,0:T(2,128)}), f32[8,2,512]{2,1,0:T(2,128)S(1)}, u32[]{:S(2)}, u32[]{:S(2)}) async-start(f32[8,2,512]{2,1,0:T(2,128)} %broadcast_in_dim.71), calls=%async_computation.3 | async-start | bytes 65536 | tf_op jit(solution)/shard_map/all_to_all | solution.py:229
  346.8 0.7 fusion.90
  347.4 7.4 %all-to-all-done.2 = f32[8,2,512]{2,1,0:T(2,128)S(1)} async-done(((f32[8,2,512]{2,1,0:T(2,128)}), f32[8,2,512]{2,1,0:T(2,128)S(1)}, u32[]{:S(2)}, u32[]{:S(2)}) %all-to-all-start.2) | async-done | bytes 32800 | tf_op jit(solution)/shard_map/all_to_all | solution.py:229
  354.8 1.9 add_convert_fusion.1
  (69 shorter events, 1.7 us)
Async XLA Ops:
  7.2 286.2 %copy-start = (bf16[512,2048]{1,0:T(8,128)(2,1)S(1)}, bf16[512,2048]{1,0:T(8,128)(2,1)}, u32[]{:S(2)}) copy-start(bf16[512,2048]{1,0:T(8,128)(2,1)} %param.42) | copy-start | bytes 6291460
  14.3 7.8 %copy-start.7 = (s32[256]{0:T(256)S(1)}, s32[256]{0:T(256)}, u32[]{:S(2)}) copy-start(s32[256]{0:T(256)} %param.25) | copy-start | bytes 3076
  14.3 9.0 %copy-start.10 = (s32[8]{0:T(128)S(1)}, s32[8]{0:T(128)}, u32[]{:S(2)}) copy-start(s32[8]{0:T(128)} %param.26) | copy-start | bytes 100
  14.3 9.0 %copy-start.8 = (s32[8,64]{1,0:T(8,128)S(1)}, s32[8,64]{1,0:T(8,128)}, u32[]{:S(2)}) copy-start(s32[8,64]{1,0:T(8,128)} %param.24) | copy-start | bytes 6148
  14.3 33.8 %all-to-all-start = ((bf16[64,64,256]{2,1,0:T(8,128)(2,1)}), bf16[64,64,256]{2,1,0:T(8,128)(2,1)}, u32[]{:S(2)}, u32[]{:S(2)}) async-start(bf16[64,64,256]{2,1,0:T(8,128)(2,1)} %bitcast.166), calls=%async_computation | async-start | bytes 4194304 | tf_op jit(solution)/shard_map/all_to_all | solution.py:144
  52.8 1.6 copy-start.11
  58.9 36.6 %all-to-all-start.1 = ((bf16[64,66,256]{2,1,0:T(8,128)(2,1)}), bf16[64,66,256]{2,1,0:T(8,128)(2,1)}, u32[]{:S(2)}, u32[]{:S(2)}) async-start(bf16[64,66,256]{2,1,0:T(8,128)(2,1)} %pad_maximum_fusion), calls=%async_computation.1 | async-start | bytes 4718592 | tf_op jit(solution)/shard_map/all_to_all | solution.py:188
  66.6 209.8 %all-gather.3.cloned.1.call-start = ((), (), s32[]{:S(2)}) async-start(), calls=%async_computation.6 | async-start | bytes 18874368 | tf_op jit(solution)/shard_map/all_gather | solution.py:209
  69.0 3.4 copy-start.13
  97.9 2.1 copy-start.3
  102.1 238.2 %reduce-scatter.2.cloned.1.call-start = ((), (), s32[]{:S(2)}) async-start(), calls=%async_computation.5 | async-start | bytes 2359296 | tf_op jit(solution)/shard_map/reduce_scatter | solution.py:217
  276.4 10.8 %copy-start.4 = (f32[2048]{0:T(1024)S(1)}, f32[2048]{0:T(1024)}, u32[]{:S(2)}) copy-start(f32[2048]{0:T(1024)} %param.37) | copy-start | bytes 24580
  287.2 3.5 copy-start.1
  287.2 3.5 copy-start.2
  287.2 3.5 copy-start.5
  287.2 3.5 copy-start.6
  290.8 2.6 copy-start.12
  299.5 0.7 copy-start.9
  299.5 2.6 copy-start.14
  304.0 21.9 %all-to-all-start.3 = ((bf16[64,32,256]{2,1,0:T(8,128)(2,1)}), bf16[64,32,256]{2,1,0:T(8,128)(2,1)S(1)}, u32[]{:S(2)}, u32[]{:S(2)}) async-start(bf16[64,32,256]{2,1,0:T(8,128)(2,1)} %bitcast.48), calls=%async_computation.4 | async-start | bytes 2097152 | tf_op jit(solution)/shard_map/all_to_all | solution.py:147
  342.2 12.6 %all-to-all-start.2 = ((f32[8,2,512]{2,1,0:T(2,128)}), f32[8,2,512]{2,1,0:T(2,128)S(1)}, u32[]{:S(2)}, u32[]{:S(2)}) async-start(f32[8,2,512]{2,1,0:T(2,128)} %broadcast_in_dim.71), calls=%async_computation.3 | async-start | bytes 65536 | tf_op jit(solution)/shard_map/all_to_all | solution.py:229
Sparse Core Ops, SparseCore 0:
  102.2 174.1 all-gather.2
  299.6 40.6 reduce-scatter.1
